TPU v7x, 256 devices: a whole 4x4x8 slice. The times are simulated.
256 devices in a mesh: dp: 4 (over z_hi), expert: 16 (over y, z_lo, core), mp: 4 (over x).
Axes of the slice: x: 4, y: 4, z: 8 (z_hi: 4, z_lo: 2; z = z_hi * 2 + z_lo), core: 2. Of those that a mesh axis runs over, the one named last changes fastest.
Arguments:
- hidden: bfloat16 [16384, 2048], P(('dp', 'expert', 'mp')), may hold values from -6 to 6
- norm_gain: float32 [2048], replicated, may hold values from 0.1 to 1.9
- expert_in: float32 [64, 2048, 2816], P('dp', ('expert', 'mp')), may hold values from -0.125 to 0.125
- expert_out: float32 [64, 2048, 1408], P('dp', ('expert', 'mp')), may hold values from -0.15625 to 0.15625
- expert_ids: int32 [16384, 6], P(('dp', 'expert', 'mp')), may hold values from 0 to 63, all different within a row; in each aligned block of 64 rows (0 to 63, 64 to 127, ...) at most 12 rows name the same one
- gate_levels: int32 [16384, 6], P(('dp', 'expert', 'mp')), may hold values from 1 to 255
- shared_gate: bfloat16 [2048, 2816], P(('dp', 'expert'), 'mp'), may hold values from -0.125 to 0.125
- shared_up: bfloat16 [2048, 2816], P(('dp', 'expert'), 'mp'), may hold values from -0.125 to 0.125
- shared_down: bfloat16 [2048, 2816], P(('dp', 'expert'), 'mp'), may hold values from -0.109375 to 0.109375
- next_gain: float32 [2048], replicated, may hold values from 0.1 to 1.9
- kv_weight: bfloat16 [2048, 576], P(None, 'mp'), may hold values from -0.125 to 0.125
Outputs:
- layer_out: bfloat16 [16384, 2048], P(('dp', 'expert', 'mp'))
- kv_latent: bfloat16 [16384, 576], P(('dp', 'expert'), 'mp')
Inputs may be any that keep to these rules, and one draw needn't show every extreme that they name: `expert_ids`: each row names 6 different experts. Among the 64 rows of one device no expert is named by more than 12 rows, and in every draw some expert is named by exactly 12 rows of some device.
All inputs are finite; a program needn't handle non-finite values.
Results may differ from a plain program's by a relative error of at most 0.012.
Values may be sent and summed in bfloat16 or wider, within the bound.
No kernel may reach another device: no remote copies, remote signals or barrier semaphores. Data moves between devices by JAX's collectives and lax.ppermute only.
A program may use at most 128 MiB of HBM per device.

v0:
```python
import jax
import jax.numpy as jnp
from jax import lax
from jax.sharding import PartitionSpec as P


def rms_scale(values, gain):
    wide = values.astype(jnp.float32)
    mean_sq = jnp.mean(wide * wide, axis=-1, keepdims=True)
    return (wide * lax.rsqrt(mean_sq + 1e-06) * gain).astype(jnp.bfloat16)


def expert_part(rows, gate_up_w, down_w):
    quarter = down_w.shape[1]
    gate_up = jnp.dot(rows, gate_up_w, preferred_element_type=jnp.float32)
    act = (jax.nn.silu(gate_up[:, :quarter]) * gate_up[:, quarter:]).astype(jnp.bfloat16)
    return lax.dot_general(
        act, down_w, (((1,), (1,)), ((), ())), preferred_element_type=jnp.float32
    )


def on_device(
    hidden,
    norm_gain,
    expert_in,
    expert_out,
    expert_ids,
    gate_levels,
    shared_gate,
    shared_up,
    shared_down,
    next_gain,
    kv_weight,
):
    tok_rows, width = hidden.shape
    top = expert_ids.shape[1]
    n_mp = lax.axis_size("mp")
    n_groups = lax.axis_size(("dp", "expert"))
    capacity = min(tok_rows, (2 * tok_rows * top + n_groups - 1) // n_groups)
    local_e, local_rows, double = expert_in.shape
    full_ff = double // 2
    quarter = full_ff // n_mp
    in_cast = (
        expert_in.astype(jnp.bfloat16)
        .reshape(local_e, local_rows, 2, n_mp, quarter)
        .transpose(0, 3, 1, 2, 4)
    )
    out_cast = (
        expert_out.astype(jnp.bfloat16)
        .reshape(local_e, local_rows, n_mp, quarter)
        .transpose(0, 2, 1, 3)
    )
    in_send = in_cast.reshape(local_e * n_mp, local_rows, 2, quarter)
    out_send = out_cast.reshape(local_e * n_mp, local_rows, quarter)
    in_recv, out_recv = (
        lax.all_to_all(in_send, ("expert", "mp"), split_axis=0, concat_axis=1, tiled=True),
        lax.all_to_all(out_send, ("expert", "mp"), split_axis=0, concat_axis=1, tiled=True),
    )
    gate_up_w = in_recv.reshape(width, 2 * quarter)
    down_w = out_recv.reshape(width, quarter)
    normed = rms_scale(hidden, norm_gain)
    levels = gate_levels.astype(jnp.float32)
    gate_weights = levels / jnp.sum(levels, axis=1, keepdims=True)
    flat_ids = expert_ids.reshape(-1)
    pairs = flat_ids.shape[0]
    onehot = (flat_ids[:, None] == jnp.arange(n_groups, dtype=jnp.int32)[None, :]).astype(jnp.int32)
    before = jnp.cumsum(onehot, axis=0) - onehot
    slot_of_pair = jnp.sum(before * onehot, axis=1)
    target = flat_ids * capacity + slot_of_pair
    token_of_pair = jnp.arange(pairs, dtype=jnp.int32) // top
    send = (
        jnp.zeros((n_groups * capacity, width), jnp.bfloat16).at[target].set(normed[token_of_pair])
    )
    received = lax.all_to_all(
        send.reshape(n_groups, capacity, width),
        ("dp", "expert"),
        split_axis=0,
        concat_axis=0,
        tiled=True,
    )
    slots_here = received.reshape(n_groups * capacity, width)
    every_slot = lax.all_gather(slots_here, "mp", axis=0, tiled=True)
    rows = every_slot
    summed = lax.psum_scatter(
        expert_part(rows, gate_up_w, down_w).astype(jnp.bfloat16),
        "mp",
        scatter_dimension=0,
        tiled=True,
    )
    result = summed.reshape(n_groups, capacity, width)
    back = lax.all_to_all(
        result, ("dp", "expert"), split_axis=0, concat_axis=0, tiled=True
    ).reshape(n_groups * capacity, width)
    picked = back[target].reshape(tok_rows, top, width)
    routed = jnp.sum(picked.astype(jnp.float32) * gate_weights[:, :, None], axis=1)
    shared_cols = shared_gate.shape[1]
    shared_cat = jnp.concatenate([shared_gate, shared_up, shared_down], axis=1)
    shared_cat = lax.all_gather(shared_cat, "dp", axis=0, tiled=False)
    shared_cat = lax.all_gather(shared_cat, "expert", axis=1, tiled=False)
    shared_cat = shared_cat.reshape(width, 3 * shared_cols)
    gate_w = shared_cat[:, :shared_cols]
    up_w = shared_cat[:, shared_cols : 2 * shared_cols]
    down_s = shared_cat[:, 2 * shared_cols :]
    group_rows = lax.all_gather(normed, "mp", axis=0, tiled=True)
    rows = group_rows
    gate_part = jnp.dot(rows, gate_w, preferred_element_type=jnp.float32)
    up_part = jnp.dot(rows, up_w, preferred_element_type=jnp.float32)
    act = (jax.nn.silu(gate_part) * up_part).astype(jnp.bfloat16)
    shared_out = lax.psum_scatter(
        lax.dot_general(act, down_s, (((1,), (1,)), ((), ())), preferred_element_type=jnp.float32),
        "mp",
        scatter_dimension=0,
        tiled=True,
    )
    layer_out = (hidden.astype(jnp.float32) + routed + shared_out).astype(jnp.bfloat16)
    next_rows = rms_scale(layer_out, next_gain)
    next_group = lax.all_gather(next_rows, "mp", axis=0, tiled=True)
    kv_latent = jnp.dot(next_group, kv_weight, preferred_element_type=jnp.float32).astype(
        jnp.bfloat16
    )
    return (layer_out, kv_latent)


def solution(mesh):
    in_specs = (
        P(("dp", "expert", "mp"), None),
        P(),
        P("dp", ("expert", "mp"), None),
        P("dp", ("expert", "mp"), None),
        P(("dp", "expert", "mp"), None),
        P(("dp", "expert", "mp"), None),
        P(("dp", "expert"), "mp"),
        P(("dp", "expert"), "mp"),
        P(("dp", "expert"), "mp"),
        P(),
        P(None, "mp"),
    )
    out_specs = (P(("dp", "expert", "mp"), None), P(("dp", "expert"), "mp"))
    return jax.shard_map(
        on_device, mesh=mesh, in_specs=in_specs, out_specs=out_specs, check_vma=False
    )
```

profile of v0, /device:TPU:1, one launch (start us, length us, event | category | flops | bytes accessed | tf_op | source)
XLA Modules:
  0.0 692.3 jit_solution(3124470099262172469)
XLA Ops:
  12.9 10.0 %scatter_custom_fusion = bf16[768,2048]{1,0:T(8,128)(2,1)} fusion(s32[384]{0:T(512)S(1)} %fusion.38, bf16[64,2048]{1,0:T(8,128)(2,1)S(1)} %fusion.30, s32[1024]{0:T(1024)S(1)} %pad_clamp_fusion.1, bf16[]{:T(256)} %constant.12.clone.1), kind=kCustom, calls=%fused_computation.15 | custom fusion | bytes 3145730 | tf_op jit(solution)/shard_map/scatter | solution.py:72
  22.8 6.1 reshape.156
  28.9 108.9 %all_to_all.28 = bf16[64,12,2048]{2,1,0:T(8,128)(2,1)} all-to-all(bf16[64,12,2048]{2,1,0:T(8,128)(2,1)} %reshape.156), channel_id=1, replica_groups=mesh['dp'=4,'expert'=16,'mp'=4] {'dp','expert'}, dimensions={0} | all-to-all | bytes 6291456 | tf_op jit(solution)/shard_map/all_to_all | solution.py:74
  137.8 6.2 reshape.157
  144.0 3.0 convert_element_type.54
  147.0 5.1 reshape.158
  152.1 4.8 copy.24
  156.9 9.3 %all-to-all-start.1 = ((bf16[64,32,2,352]{3,1,2,0:T(8,128)(2,1)}), bf16[64,32,2,352]{3,1,2,0:T(8,128)(2,1)}, u32[]{:S(2)}, u32[]{:S(2)}) async-start(bf16[64,32,2,352]{3,1,2,0:T(8,128)(2,1)} %bitcast.33), calls=%async_computation.1 | async-start | bytes 6291456 | tf_op jit(solution)/shard_map/all_to_all | solution.py:56
  166.9 1.4 pad_maximum_fusion
  168.3 54.8 %all-to-all-done.1 = bf16[64,32,2,352]{3,1,2,0:T(8,128)(2,1)} async-done(((bf16[64,32,2,352]{3,1,2,0:T(8,128)(2,1)}), bf16[64,32,2,352]{3,1,2,0:T(8,128)(2,1)}, u32[]{:S(2)}, u32[]{:S(2)}) %all-to-all-start.1) | async-done | bytes 2883616 | tf_op jit(solution)/shard_map/all_to_all | solution.py:56
  223.1 4.4 all-to-all-start.2
  227.5 6.9 copy.25
  234.4 7.8 %reshape.160 = bf16[2048,704]{1,0:T(8,128)(2,1)} reshape(bf16[64,32,2,352]{3,2,1,0:T(2,128)(2,1)} %copy.25) | data formatting | bytes 5767168 | tf_op jit(solution)/shard_map/reshape | solution.py:59
  242.2 70.8 %all-gather.7.cloned.1.call-done = bf16[3072,2048]{1,0:T(8,128)(2,1)} async-done(((bf16[768,2048]{1,0:T(8,128)(2,1)}), bf16[3072,2048]{1,0:T(8,128)(2,1)}) %all-gather.7.cloned.1.call-update) | async-done | bytes 12582928 | tf_op jit(solution)/shard_map/all_gather | solution.py:82
  312.9 15.1 %fusion.44 = f32[3072,704]{0,1:T(8,128)} fusion(bf16[3072,2048]{1,0:T(8,128)(2,1)} %all-gather.7.cloned.1.call-done, bf16[2048,704]{1,0:T(8,128)(2,1)} %reshape.160), kind=kOutput, calls=%fused_computation.67 | convolution fusion | flops 8858370048 | bytes 24117248 | tf_op jit(solution)/shard_map/dot_general | solution.py:15
  328.1 13.5 %convolution_convert_fusion = bf16[3072,2048]{1,0:T(8,128)(2,1)} fusion(bf16[2048,352]{1,0:T(8,128)(2,1)S(1)} %bitcast.36, f32[3072,704]{0,1:T(8,128)} %fusion.44), kind=kOutput, calls=%fused_computation.3 | convolution fusion | flops 4441964544 | bytes 22675456 | tf_op jit(solution)/shard_map/dot_general | solution.py:17
  342.5 17.1 %all-gather = bf16[128,2112]{1,0:T(8,128)(2,1)} all-gather(bf16[32,2112]{1,0:T(8,128)(2,1)S(1)} %concatenate.7), channel_id=2, replica_groups=mesh['dp'=4,'expert'=16,'mp'=4] {'dp'}, dimensions={0}, use_global_device_ids=true | all-gather | bytes 675840 | tf_op jit(solution)/shard_map/all_gather | solution.py:98
  359.7 100.2 %reduce-scatter.3.cloned.1.call-done = bf16[768,2048]{1,0:T(8,128)(2,1)} async-done(((bf16[3072,2048]{1,0:T(8,128)(2,1)}), bf16[768,2048]{1,0:T(8,128)(2,1)}) %reduce-scatter.3.cloned.1.call-update) | async-done | bytes 3145744 | tf_op jit(solution)/shard_map/reduce_scatter | solution.py:84
  459.9 6.1 reshape.163
  466.0 10.8 %all-to-all-start.3 = ((bf16[64,12,2048]{2,1,0:T(8,128)(2,1)}), bf16[64,12,2048]{2,1,0:T(8,128)(2,1)}, u32[]{:S(2)}, u32[]{:S(2)}) async-start(bf16[64,12,2048]{2,1,0:T(8,128)(2,1)} %reshape.163), calls=%async_computation.4 | async-start | bytes 8388608 | tf_op jit(solution)/shard_map/all_to_all | solution.py:91
  477.1 10.5 %all-gather.9.cloned.1.call-done = bf16[256,2048]{1,0:T(8,128)(2,1)} async-done(((bf16[64,2048]{1,0:T(8,128)(2,1)}), bf16[256,2048]{1,0:T(8,128)(2,1)}) %all-gather.9.cloned.1.call-update) | async-done | bytes 1048592 | tf_op jit(solution)/shard_map/all_gather | solution.py:104
  487.6 125.0 %all-gather.13.cloned.1.call-done = bf16[4,512,2112]{2,1,0:T(8,128)(2,1)} async-done(((bf16[4,32,2112]{2,1,0:T(8,128)(2,1)}), bf16[4,512,2112]{2,1,0:T(8,128)(2,1)}) %all-gather.13.cloned.1.call-update) | async-done | bytes 8650768 | tf_op jit(solution)/shard_map/all_gather | solution.py:99
  612.6 3.5 fusion.5
  616.2 8.8 %fusion.1 = f32[256,2048]{1,0:T(8,128)} fusion(bf16[2048,2112]{1,0:T(8,128)(2,1)} %bitcast.39, bf16[256,2048]{1,0:T(8,128)(2,1)S(1)} %copy-done.10, f32[256,704]{0,1:T(8,128)S(1)} %fusion.5), kind=kOutput, calls=%fused_computation.7 | convolution fusion | flops 1477476352 | bytes 10158080 | tf_op jit(solution)/shard_map/dot_general | solution.py:110
  625.1 6.2 reshape.164
  631.3 6.7 gather_fusion
  638.0 2.2 reshape.166
  640.2 3.8 multiply_reduce_fusion
  644.0 11.2 %reduce-scatter.5.cloned.1.call-done = f32[64,2048]{1,0:T(8,128)} async-done(((f32[256,2048]{1,0:T(8,128)}), f32[64,2048]{1,0:T(8,128)}) %reduce-scatter.5.cloned.1.call-update) | async-done | bytes 524304 | tf_op jit(solution)/shard_map/reduce_scatter | solution.py:109
  655.3 1.2 fusion.25
  657.4 25.5 %all-gather.11.cloned.1.call-done = bf16[256,2048]{1,0:T(8,128)(2,1)} async-done(((bf16[64,2048]{1,0:T(8,128)(2,1)}), bf16[256,2048]{1,0:T(8,128)(2,1)}) %all-gather.11.cloned.1.call-update) | async-done | bytes 1048592 | tf_op jit(solution)/shard_map/all_gather | solution.py:117
  682.9 2.4 convolution_convert_fusion.1
  (62 shorter events, 8.6 us)
Async XLA Ops:
  7.2 675.7 %copy-start = (bf16[2048,144]{0,1:T(8,128)(2,1)S(1)}, bf16[2048,144]{0,1:T(8,128)(2,1)}, u32[]{:S(2)}) copy-start(bf16[2048,144]{0,1:T(8,128)(2,1)} %param.21) | copy-start | bytes 1769476
  7.2 305.8 %all-gather.7.cloned.1.call-start = ((), (), s32[]{:S(2)}) async-start(), calls=%async_computation.6 | async-start | bytes 15728640 | tf_op jit(solution)/shard_map/all_gather | solution.py:82
  12.9 16.1 %copy-start.3 = (bf16[64,2048]{1,0:T(8,128)(2,1)}, bf16[64,2048]{1,0:T(8,128)(2,1)S(1)}, u32[]{:S(2)}) copy-start(bf16[64,2048]{1,0:T(8,128)(2,1)S(1)} %fusion.30) | copy-start | bytes 786436
  156.9 9.3 %copy-start.1 = (f32[16,32,1408]{2,1,0:T(8,128)S(1)}, f32[16,32,1408]{2,1,0:T(8,128)}, u32[]{:S(2)}) copy-start(f32[16,32,1408]{2,1,0:T(8,128)} %param.14) | copy-start | bytes 8650756
  156.9 66.2 %all-to-all-start.1 = ((bf16[64,32,2,352]{3,1,2,0:T(8,128)(2,1)}), bf16[64,32,2,352]{3,1,2,0:T(8,128)(2,1)}, u32[]{:S(2)}, u32[]{:S(2)}) async-start(bf16[64,32,2,352]{3,1,2,0:T(8,128)(2,1)} %bitcast.33), calls=%async_computation.1 | async-start | bytes 6291456 | tf_op jit(solution)/shard_map/all_to_all | solution.py:56
  223.1 105.0 %all-to-all-start.2 = ((bf16[64,32,352]{2,1,0:T(8,128)(2,1)}), bf16[64,32,352]{2,1,0:T(8,128)(2,1)S(1)}, u32[]{:S(2)}, u32[]{:S(2)}) async-start(bf16[64,32,352]{2,1,0:T(8,128)(2,1)} %bitcast.3), calls=%async_computation.2 | async-start | bytes 3145728 | tf_op jit(solution)/shard_map/all_to_all | solution.py:57
  227.4 232.4 %reduce-scatter.3.cloned.1.call-start = ((), (), s32[]{:S(2)}) async-start(), calls=%async_computation.7 | async-start | bytes 15728640 | tf_op jit(solution)/shard_map/reduce_scatter | solution.py:84
  341.6 0.8 copy-start.5
  341.6 0.8 copy-start.6
  341.6 0.8 copy-start.7
  341.6 146.0 %all-gather.9.cloned.1.call-start = ((), (), s32[]{:S(2)}) async-start(), calls=%async_computation.8 | async-start | bytes 1310720 | tf_op jit(solution)/shard_map/all_gather | solution.py:104
  342.3 270.3 %all-gather.13.cloned.1.call-start = ((), (), s32[]{:S(2)}) async-start(), calls=%async_computation.11 | async-start | bytes 9469952 | tf_op jit(solution)/shard_map/all_gather | solution.py:99
  466.0 159.2 %all-to-all-start.3 = ((bf16[64,12,2048]{2,1,0:T(8,128)(2,1)}), bf16[64,12,2048]{2,1,0:T(8,128)(2,1)}, u32[]{:S(2)}, u32[]{:S(2)}) async-start(bf16[64,12,2048]{2,1,0:T(8,128)(2,1)} %reshape.163), calls=%async_computation.4 | async-start | bytes 8388608 | tf_op jit(solution)/shard_map/all_to_all | solution.py:91
  476.8 178.4 %reduce-scatter.5.cloned.1.call-start = ((), (), s32[]{:S(2)}) async-start(), calls=%async_computation.9 | async-start | bytes 2621440 | tf_op jit(solution)/shard_map/reduce_scatter | solution.py:109
  487.6 128.5 %copy-start.10 = (bf16[256,2048]{1,0:T(8,128)(2,1)S(1)}, bf16[256,2048]{1,0:T(8,128)(2,1)}, u32[]{:S(2)}) copy-start(bf16[256,2048]{1,0:T(8,128)(2,1)} %all-gather.9.cloned.1.call-done) | copy-start | bytes 3145732
  616.1 8.8 %copy-start.8 = (s32[64,6]{0,1:T(8,128)S(1)}, s32[64,6]{0,1:T(8,128)}, u32[]{:S(2)}) copy-start(s32[64,6]{0,1:T(8,128)} %param.16) | copy-start | bytes 4612
  624.9 57.9 %all-gather.11.cloned.1.call-start = ((), (), s32[]{:S(2)}) async-start(), calls=%async_computation.10 | async-start | bytes 1310720 | tf_op jit(solution)/shard_map/all_gather | solution.py:117
  640.2 15.1 %copy-start.2 = (bf16[64,2048]{1,0:T(8,128)(2,1)S(1)}, bf16[64,2048]{1,0:T(8,128)(2,1)}, u32[]{:S(2)}) copy-start(bf16[64,2048]{1,0:T(8,128)(2,1)} %param.11) | copy-start | bytes 786436
  640.2 16.3 %copy-start.9 = (f32[2048]{0:T(1024)S(1)}, f32[2048]{0:T(1024)}, u32[]{:S(2)}) copy-start(f32[2048]{0:T(1024)} %param.20) | copy-start | bytes 24580
  656.5 28.7 %copy-start.4 = (bf16[64,2048]{1,0:T(8,128)(2,1)}, bf16[64,2048]{1,0:T(8,128)(2,1)S(1)}, u32[]{:S(2)}) copy-start(bf16[64,2048]{1,0:T(8,128)(2,1)S(1)} %get-tuple-element.3) | copy-start | bytes 786436
Sparse Core Ops, SparseCore 0:
  144.1 168.7 all-gather.6
  341.7 118.1 reduce-scatter.2
  462.3 25.2 all-gather.8
  489.3 123.3 all-gather.12
  625.1 30.1 reduce-scatter.4
  657.5 25.2 all-gather.10
where the time goes:
time: 702 us; the launch traced here: 692 us
  waiting for transfers between devices  399 us (57%)
  blocking collectives  126 us (18%)
  local copies, waits for them, and re-layouts  70.2 us (10%)
  matrix products  43.2 us (6%)
  starting transfers between devices  25 us (4%)
  between operations  14.6 us (2%)
  other arithmetic  14.5 us (2%)
    all_gather x1, waiting for transfers between devices, on_device(): shared_cat = lax.all_gather(shared_cat, 'expert', axis=1, tiled=False)  125 us
    all_to_all x1, blocking collectives, on_device(): lax.all_to_all(send.reshape(n_groups, capacity, width), ('dp', 'expert'),...  109 us
    reduce_scatter x1, waiting for transfers between devices, on_device(): lax.psum_scatter(expert_part(rows, gate_up_w, down_w).astype(jnp.bfloat16...  100 us
    all_gather x1, waiting for transfers between devices, on_device(): every_slot = lax.all_gather(slots_here, 'mp', axis=0, tiled=True)  70.8 us
    all_to_all x1, waiting for transfers between devices, on_device(): lax.all_to_all(in_send, ('expert', 'mp'), split_axis=0, concat_axis=1, ti...  54.8 us
    all_gather x1, waiting for transfers between devices, on_device(): next_group = lax.all_gather(next_rows, 'mp', axis=0, tiled=True)  25.5 us
    all_gather x1, blocking collectives, on_device(): shared_cat = lax.all_gather(shared_cat, 'dp', axis=0, tiled=False)  17.1 us
    dot_general x1, matrix products, expert_part(): gate_up = jnp.dot(rows, gate_up_w, preferred_element_type=jnp.float32)  15.1 us
  transfers between devices with their start and end apart: 9, of which 7 were waited for; matrix products, arithmetic and copies ran while one was open for 12% of the time, Pallas kernels for 0%

commit v1 on v0

--- a/solution.py
+++ b/solution.py
@@ -79,7 +79,9 @@
         tiled=True,
     )
     slots_here = received.reshape(n_groups * capacity, width)
-    every_slot = lax.all_gather(slots_here, "mp", axis=0, tiled=True)
+    every_slot = jnp.concatenate(
+        lax.all_to_all(jnp.stack([slots_here] * lax.axis_size("mp")), "mp", 0, 0), axis=0
+    )
     rows = every_slot
     summed = lax.psum_scatter(
         expert_part(rows, gate_up_w, down_w).astype(jnp.bfloat16),

time: 702 us -> 745 us (1.061)
  waiting for transfers between devices: 399 us -> 525 us
  blocking collectives: 126 us -> 13.5 us
  starting transfers between devices: 25 us -> 47.1 us
  local copies, waits for them, and re-layouts: 70.2 us -> 77.8 us
    all_to_all x0 -> x2, waiting for transfers between devices: none -> 218 us  [the longest x1 137 us: on_device(): lax.all_to_all(jnp.stack([slots_here] * lax.axis_size('mp')), 'mp', 0, 0)]
    all_to_all x1 -> x0, blocking collectives: 109 us -> none  [on_device(): lax.all_to_all(send.reshape(n_groups, capacity, width), ('dp', 'expert'),...]
    all_gather x1 -> x0, waiting for transfers between devices: 70.8 us -> none  [on_device(): every_slot = lax.all_gather(slots_here, 'mp', axis=0, tiled=True)]
    all_to_all x0 -> x2, starting transfers between devices: none -> 20.6 us  [the longest x1 14 us: on_device(): lax.all_to_all(send.reshape(n_groups, capacity, width), ('dp', 'expert'),...]
    all_to_all x1, waiting for transfers between devices: 54.8 us -> 34.6 us  [on_device(): lax.all_to_all(in_send, ('expert', 'mp'), split_axis=0, concat_axis=1, ti...]
    another operation x1 -> x3, local copies, waits for them, and re-layouts: 0.48 us -> 14.8 us  [the longest x2 14.3 us: on_device(): jnp.stack([slots_here] * lax.axis_size('mp'))]
  transfers between devices with their start and end apart: 9 -> 10, of which waited for: 7 -> 8; matrix products, arithmetic and copies ran while one was open for 12% -> 12% of each run, Pallas kernels for 0% -> 0%
where the time goes in v1:
time: 745 us; the launch traced here: 736 us
  waiting for transfers between devices  525 us (70%)
  local copies, waits for them, and re-layouts  77.8 us (10%)
  starting transfers between devices  47.1 us (6%)
  matrix products  43.2 us (6%)
  other arithmetic  14.6 us (2%)
  between operations  14.3 us (2%)
  blocking collectives  13.5 us (2%)
    all_to_all x1, waiting for transfers between devices, on_device(): lax.all_to_all(jnp.stack([slots_here] * lax.axis_size('mp')), 'mp', 0, 0)  137 us
    all_gather x1, waiting for transfers between devices, on_device(): shared_cat = lax.all_gather(shared_cat, 'expert', axis=1, tiled=False)  125 us
    reduce_scatter x1, waiting for transfers between devices, on_device(): lax.psum_scatter(expert_part(rows, gate_up_w, down_w).astype(jnp.bfloat16...  99.9 us
    all_to_all x1, waiting for transfers between devices, on_device(): lax.all_to_all(send.reshape(n_groups, capacity, width), ('dp', 'expert'),...  81.4 us
    all_to_all x1, waiting for transfers between devices, on_device(): lax.all_to_all(in_send, ('expert', 'mp'), split_axis=0, concat_axis=1, ti...  34.6 us
    all_gather x1, waiting for transfers between devices, on_device(): next_group = lax.all_gather(next_rows, 'mp', axis=0, tiled=True)  25.5 us
    dot_general x1, matrix products, expert_part(): gate_up = jnp.dot(rows, gate_up_w, preferred_element_type=jnp.float32)  15.2 us
  transfers between devices with their start and end apart: 10, of which 8 were waited for; matrix products, arithmetic and copies ran while one was open for 12% of the time, Pallas kernels for 0%

profile of v1, /device:TPU:1, one launch (start us, length us, event | category | flops | bytes accessed | tf_op | source)
XLA Modules:
  0.0 735.9 jit_solution(16102995361787878350)
XLA Ops:
  12.8 10.0 %scatter_custom_fusion = bf16[768,2048]{1,0:T(8,128)(2,1)} fusion(s32[384]{0:T(512)S(1)} %fusion.38, bf16[64,2048]{1,0:T(8,128)(2,1)S(1)} %fusion.30, s32[1024]{0:T(1024)S(1)} %pad_clamp_fusion.1, bf16[]{:T(256)} %constant.12.clone.1), kind=kCustom, calls=%fused_computation.15 | custom fusion | bytes 3145730 | tf_op jit(solution)/shard_map/scatter | solution.py:72
  22.8 6.1 reshape.158
  28.9 14.0 %all-to-all-start = ((bf16[64,12,2048]{2,1,0:T(8,128)(2,1)}), bf16[64,12,2048]{2,1,0:T(8,128)(2,1)}, u32[]{:S(2)}, u32[]{:S(2)}) async-start(bf16[64,12,2048]{2,1,0:T(8,128)(2,1)} %reshape.158), calls=%async_computation | async-start | bytes 8388608 | tf_op jit(solution)/shard_map/all_to_all | solution.py:74
  42.9 3.0 convert_element_type.54
  45.9 5.0 reshape.160
  50.9 4.4 copy.24
  55.3 81.4 %all-to-all-done = bf16[64,12,2048]{2,1,0:T(8,128)(2,1)} async-done(((bf16[64,12,2048]{2,1,0:T(8,128)(2,1)}), bf16[64,12,2048]{2,1,0:T(8,128)(2,1)}, u32[]{:S(2)}, u32[]{:S(2)}) %all-to-all-start) | async-done | bytes 3145760 | tf_op jit(solution)/shard_map/all_to_all | solution.py:74
  136.7 10.1 %all-to-all-start.2 = ((bf16[64,32,2,352]{3,1,2,0:T(8,128)(2,1)}), bf16[64,32,2,352]{3,1,2,0:T(8,128)(2,1)}, u32[]{:S(2)}, u32[]{:S(2)}) async-start(bf16[64,32,2,352]{3,1,2,0:T(8,128)(2,1)} %bitcast.34), calls=%async_computation.2 | async-start | bytes 6291456 | tf_op jit(solution)/shard_map/all_to_all | solution.py:56
  146.9 6.2 stack_reshape.2
  153.0 34.6 %all-to-all-done.2 = bf16[64,32,2,352]{3,1,2,0:T(8,128)(2,1)} async-done(((bf16[64,32,2,352]{3,1,2,0:T(8,128)(2,1)}), bf16[64,32,2,352]{3,1,2,0:T(8,128)(2,1)}, u32[]{:S(2)}, u32[]{:S(2)}) %all-to-all-start.2) | async-done | bytes 2883616 | tf_op jit(solution)/shard_map/all_to_all | solution.py:56
  187.6 8.1 %stack.3 = bf16[4,768,2048]{2,1,0:T(8,128)(2,1)} broadcast(bf16[768,2048]{1,0:T(8,128)(2,1)} %stack_reshape.2), dimensions={1,2} | broadcast | bytes 15728640 | tf_op jit(solution)/shard_map/stack | solution.py:83
  195.8 6.6 all-to-all-start.1
  204.4 136.6 %all-to-all-done.1 = bf16[4,768,2048]{2,1,0:T(8,128)(2,1)} async-done(((bf16[4,768,2048]{2,1,0:T(8,128)(2,1)}), bf16[4,768,2048]{2,1,0:T(8,128)(2,1)}, u32[]{:S(2)}, u32[]{:S(2)}) %all-to-all-start.1) | async-done | bytes 12582944 | tf_op jit(solution)/shard_map/all_to_all | solution.py:83
  341.0 5.2 all-to-all-start.3
  346.2 6.9 copy.25
  353.1 7.8 %reshape.162 = bf16[2048,704]{1,0:T(8,128)(2,1)} reshape(bf16[64,32,2,352]{3,2,1,0:T(2,128)(2,1)} %copy.25) | data formatting | bytes 5767168 | tf_op jit(solution)/shard_map/reshape | solution.py:59
  360.9 15.2 %fusion.44 = f32[3072,704]{0,1:T(8,128)} fusion(bf16[3072,2048]{1,0:T(8,128)(2,1)} %bitcast.1, bf16[2048,704]{1,0:T(8,128)(2,1)} %reshape.162), kind=kOutput, calls=%fused_computation.67 | convolution fusion | flops 8858370048 | bytes 24117248 | tf_op jit(solution)/shard_map/dot_general | solution.py:15
  376.0 13.4 %convolution_convert_fusion = bf16[3072,2048]{1,0:T(8,128)(2,1)} fusion(bf16[2048,352]{1,0:T(8,128)(2,1)S(1)} %bitcast.37, f32[3072,704]{0,1:T(8,128)} %fusion.44), kind=kOutput, calls=%fused_computation.3 | convolution fusion | flops 4441964544 | bytes 22675456 | tf_op jit(solution)/shard_map/dot_general | solution.py:17
  390.4 13.5 %all-gather = bf16[128,2112]{1,0:T(8,128)(2,1)} all-gather(bf16[32,2112]{1,0:T(8,128)(2,1)S(1)} %concatenate.7), channel_id=2, replica_groups=mesh['dp'=4,'expert'=16,'mp'=4] {'dp'}, dimensions={0}, use_global_device_ids=true | all-gather | bytes 675840 | tf_op jit(solution)/shard_map/all_gather | solution.py:100
  403.9 99.9 %reduce-scatter.3.cloned.1.call-done = bf16[768,2048]{1,0:T(8,128)(2,1)} async-done(((bf16[3072,2048]{1,0:T(8,128)(2,1)}), bf16[768,2048]{1,0:T(8,128)(2,1)}) %reduce-scatter.3.cloned.1.call-update) | async-done | bytes 3145744 | tf_op jit(solution)/shard_map/reduce_scatter | solution.py:86
  503.8 6.1 reshape.165
  509.9 10.8 %all-to-all-start.4 = ((bf16[64,12,2048]{2,1,0:T(8,128)(2,1)}), bf16[64,12,2048]{2,1,0:T(8,128)(2,1)}, u32[]{:S(2)}, u32[]{:S(2)}) async-start(bf16[64,12,2048]{2,1,0:T(8,128)(2,1)} %reshape.165), calls=%async_computation.5 | async-start | bytes 8388608 | tf_op jit(solution)/shard_map/all_to_all | solution.py:93
  521.0 10.5 %all-gather.6.cloned.1.call-done = bf16[256,2048]{1,0:T(8,128)(2,1)} async-done(((bf16[64,2048]{1,0:T(8,128)(2,1)}), bf16[256,2048]{1,0:T(8,128)(2,1)}) %all-gather.6.cloned.1.call-update) | async-done | bytes 1048592 | tf_op jit(solution)/shard_map/all_gather | solution.py:106
  531.6 125.0 %all-gather.10.cloned.1.call-done = bf16[4,512,2112]{2,1,0:T(8,128)(2,1)} async-done(((bf16[4,32,2112]{2,1,0:T(8,128)(2,1)}), bf16[4,512,2112]{2,1,0:T(8,128)(2,1)}) %all-gather.10.cloned.1.call-update) | async-done | bytes 8650768 | tf_op jit(solution)/shard_map/all_gather | solution.py:101
  656.6 3.5 fusion.5
  660.1 8.8 %fusion.1 = f32[256,2048]{1,0:T(8,128)} fusion(bf16[2048,2112]{1,0:T(8,128)(2,1)} %bitcast.40, bf16[256,2048]{1,0:T(8,128)(2,1)S(1)} %copy-done.10, f32[256,704]{0,1:T(8,128)S(1)} %fusion.5), kind=kOutput, calls=%fused_computation.7 | convolution fusion | flops 1477476352 | bytes 10158080 | tf_op jit(solution)/shard_map/dot_general | solution.py:112
  669.1 6.2 reshape.166
  675.3 6.7 gather_fusion
  684.1 3.8 multiply_reduce_fusion
  688.0 11.2 %reduce-scatter.5.cloned.1.call-done = f32[64,2048]{1,0:T(8,128)} async-done(((f32[256,2048]{1,0:T(8,128)}), f32[64,2048]{1,0:T(8,128)}) %reduce-scatter.5.cloned.1.call-update) | async-done | bytes 524304 | tf_op jit(solution)/shard_map/reduce_scatter | solution.py:111
  701.4 25.5 %all-gather.8.cloned.1.call-done = bf16[256,2048]{1,0:T(8,128)(2,1)} async-done(((bf16[64,2048]{1,0:T(8,128)(2,1)}), bf16[256,2048]{1,0:T(8,128)(2,1)}) %all-gather.8.cloned.1.call-update) | async-done | bytes 1048592 | tf_op jit(solution)/shard_map/all_gather | solution.py:119
  726.8 2.4 convolution_convert_fusion.1
  (63 shorter events, 13.4 us)
Async XLA Ops:
  7.2 719.7 %copy-start = (bf16[2048,144]{0,1:T(8,128)(2,1)S(1)}, bf16[2048,144]{0,1:T(8,128)(2,1)}, u32[]{:S(2)}) copy-start(bf16[2048,144]{0,1:T(8,128)(2,1)} %param.21) | copy-start | bytes 1769476
  12.8 16.1 %copy-start.3 = (bf16[64,2048]{1,0:T(8,128)(2,1)}, bf16[64,2048]{1,0:T(8,128)(2,1)S(1)}, u32[]{:S(2)}) copy-start(bf16[64,2048]{1,0:T(8,128)(2,1)S(1)} %fusion.30) | copy-start | bytes 786436
  28.9 107.9 %all-to-all-start = ((bf16[64,12,2048]{2,1,0:T(8,128)(2,1)}), bf16[64,12,2048]{2,1,0:T(8,128)(2,1)}, u32[]{:S(2)}, u32[]{:S(2)}) async-start(bf16[64,12,2048]{2,1,0:T(8,128)(2,1)} %reshape.158), calls=%async_computation | async-start | bytes 8388608 | tf_op jit(solution)/shard_map/all_to_all | solution.py:74
  136.7 50.9 %all-to-all-start.2 = ((bf16[64,32,2,352]{3,1,2,0:T(8,128)(2,1)}), bf16[64,32,2,352]{3,1,2,0:T(8,128)(2,1)}, u32[]{:S(2)}, u32[]{:S(2)}) async-start(bf16[64,32,2,352]{3,1,2,0:T(8,128)(2,1)} %bitcast.34), calls=%async_computation.2 | async-start | bytes 6291456 | tf_op jit(solution)/shard_map/all_to_all | solution.py:56
  195.7 6.6 copy-start.1
  195.8 145.3 %all-to-all-start.1 = ((bf16[4,768,2048]{2,1,0:T(8,128)(2,1)}), bf16[4,768,2048]{2,1,0:T(8,128)(2,1)}, u32[]{:S(2)}, u32[]{:S(2)}) async-start(bf16[4,768,2048]{2,1,0:T(8,128)(2,1)} %stack.3), calls=%async_computation.1 | async-start | bytes 25165824 | tf_op jit(solution)/shard_map/all_to_all | solution.py:83
  341.0 35.0 %all-to-all-start.3 = ((bf16[64,32,352]{2,1,0:T(8,128)(2,1)}), bf16[64,32,352]{2,1,0:T(8,128)(2,1)S(1)}, u32[]{:S(2)}, u32[]{:S(2)}) async-start(bf16[64,32,352]{2,1,0:T(8,128)(2,1)} %bitcast.4), calls=%async_computation.3 | async-start | bytes 3145728 | tf_op jit(solution)/shard_map/all_to_all | solution.py:57
  346.2 157.6 %reduce-scatter.3.cloned.1.call-start = ((), (), s32[]{:S(2)}) async-start(), calls=%async_computation.7 | async-start | bytes 15728640 | tf_op jit(solution)/shard_map/reduce_scatter | solution.py:86
  389.5 0.8 copy-start.5
  389.5 0.8 copy-start.6
  389.5 0.8 copy-start.7
  389.5 142.1 %all-gather.6.cloned.1.call-start = ((), (), s32[]{:S(2)}) async-start(), calls=%async_computation.8 | async-start | bytes 1310720 | tf_op jit(solution)/shard_map/all_gather | solution.py:106
  390.2 266.3 %all-gather.10.cloned.1.call-start = ((), (), s32[]{:S(2)}) async-start(), calls=%async_computation.11 | async-start | bytes 9469952 | tf_op jit(solution)/shard_map/all_gather | solution.py:101
  509.9 159.2 %all-to-all-start.4 = ((bf16[64,12,2048]{2,1,0:T(8,128)(2,1)}), bf16[64,12,2048]{2,1,0:T(8,128)(2,1)}, u32[]{:S(2)}, u32[]{:S(2)}) async-start(bf16[64,12,2048]{2,1,0:T(8,128)(2,1)} %reshape.165), calls=%async_computation.5 | async-start | bytes 8388608 | tf_op jit(solution)/shard_map/all_to_all | solution.py:93
  520.7 178.5 %reduce-scatter.5.cloned.1.call-start = ((), (), s32[]{:S(2)}) async-start(), calls=%async_computation.9 | async-start | bytes 2621440 | tf_op jit(solution)/shard_map/reduce_scatter | solution.py:111
  531.6 128.5 %copy-start.10 = (bf16[256,2048]{1,0:T(8,128)(2,1)S(1)}, bf16[256,2048]{1,0:T(8,128)(2,1)}, u32[]{:S(2)}) copy-start(bf16[256,2048]{1,0:T(8,128)(2,1)} %all-gather.6.cloned.1.call-done) | copy-start | bytes 3145732
  660.1 8.8 %copy-start.8 = (s32[64,6]{0,1:T(8,128)S(1)}, s32[64,6]{0,1:T(8,128)}, u32[]{:S(2)}) copy-start(s32[64,6]{0,1:T(8,128)} %param.16) | copy-start | bytes 4612
  668.9 57.9 %all-gather.8.cloned.1.call-start = ((), (), s32[]{:S(2)}) async-start(), calls=%async_computation.10 | async-start | bytes 1310720 | tf_op jit(solution)/shard_map/all_gather | solution.py:119
  684.1 15.1 %copy-start.2 = (bf16[64,2048]{1,0:T(8,128)(2,1)S(1)}, bf16[64,2048]{1,0:T(8,128)(2,1)}, u32[]{:S(2)}) copy-start(bf16[64,2048]{1,0:T(8,128)(2,1)} %param.11) | copy-start | bytes 786436
  684.1 16.4 %copy-start.9 = (f32[2048]{0:T(1024)S(1)}, f32[2048]{0:T(1024)}, u32[]{:S(2)}) copy-start(f32[2048]{0:T(1024)} %param.20) | copy-start | bytes 24580
  700.5 28.7 %copy-start.4 = (bf16[64,2048]{1,0:T(8,128)(2,1)}, bf16[64,2048]{1,0:T(8,128)(2,1)S(1)}, u32[]{:S(2)}) copy-start(bf16[64,2048]{1,0:T(8,128)(2,1)S(1)} %get-tuple-element.3) | copy-start | bytes 786436
Sparse Core Ops, SparseCore 0:
  389.6 114.1 reduce-scatter.2
  506.2 25.3 all-gather.5
  533.4 123.1 all-gather.9
  669.0 30.1 reduce-scatter.4
  701.5 25.2 all-gather.7
